TPU v7x, 32 devices: a whole 2x2x4 slice. The times are simulated.
32 devices in a mesh: nets: 8 (over z, x), region: 4 (over y, core).
Axes of the slice: x: 2, y: 2, z: 4, core: 2. Of those that a mesh axis runs over, the one named last changes fastest.
Arguments:
- logits: float32 [8192, 256], P('nets'), may hold values from -24 to 465
- tile_values: bfloat16 [8, 4, 384, 128, 128], P('nets', 'region'), may hold values from 0 to 1
- tile_pattern: int32 [8, 4, 384], P('nets', 'region'), may hold values from 0 to 2047
- tile_edge: int32 [8, 4, 384], P('nets', 'region'), may hold values from 0 to 63
- tile_counts: int32 [8, 4, 8], P('nets', 'region'), may hold values from 12 to 48, as said below
- capacity: int32 [4, 65536], P('region', 'nets'), may hold values from 0 to 2
Outputs:
- logit_grad: float32 [8192, 256], P('nets')
- usage: float32 [4, 65536], P('region', 'nets')
Inputs may be any that keep to these rules, and one draw needn't show every extreme that they name: `tile_counts`: each entry is at most 48; in every draw some owner receives 48 live slots from every group of a region, and every group has a full owner in every region.
All inputs are finite; a program needn't handle non-finite values.
Results may differ from a plain program's by a relative error of at most 0.0011.
Values may be sent and summed in bfloat16 or wider, within the bound.
No kernel may reach another device: no remote copies, remote signals or barrier semaphores. Data moves between devices by JAX's collectives and lax.ppermute only.
A program may use at most 64 MiB of HBM per device.

v0:
```python
import jax
import jax.numpy as jnp
from jax import lax
from jax.sharding import PartitionSpec as P


def shards(logits, tile_values, tile_pattern, tile_edge, tile_counts, capacity):
    groups = lax.axis_size("nets")
    tile_block = tile_values[0, 0]
    tile_count = tile_block.shape[0]
    block_size = tile_block.shape[1]
    slot_count = tile_count // groups
    pattern_idx = tile_pattern[0, 0]
    edge_idx = tile_edge[0, 0]
    counts = tile_counts[0, 0]
    live_slot = (jnp.arange(slot_count, dtype=jnp.int32)[None, :] < counts[:, None]).reshape(
        tile_count
    )
    weight_live = live_slot.astype(jnp.float32)
    probs = jax.nn.softmax(logits, axis=-1)
    probs_half = probs.astype(jnp.bfloat16).reshape(-1, block_size)
    picked = probs_half[pattern_idx]
    contrib = (
        jnp.einsum("tq,tqe->te", picked, tile_block, preferred_element_type=jnp.float32)
        * weight_live[:, None]
    )
    capacity_f = capacity.reshape(-1, block_size).astype(jnp.float32)
    owned_blocks = capacity_f.shape[0]
    owner_idx = jnp.arange(tile_count, dtype=jnp.int32) // slot_count
    target = owner_idx * owned_blocks + edge_idx
    partial_value = (
        jnp.zeros((groups * owned_blocks, block_size), jnp.float32).at[target].add(contrib)
    )
    usage_edges = lax.psum_scatter(partial_value, "nets", scatter_dimension=0, tiled=True)
    edge_grad = jax.nn.sigmoid(usage_edges - capacity_f).astype(jnp.bfloat16)
    all_grads = lax.all_gather(edge_grad, "nets", axis=0, tiled=True)
    slot_grads = all_grads[target]
    dp_tiles = (
        jnp.einsum("tqe,te->tq", tile_block, slot_grads, preferred_element_type=jnp.float32)
        * weight_live[:, None]
    )
    local_grad = (
        jnp.zeros((probs_half.shape[0], block_size), jnp.float32).at[pattern_idx].add(dp_tiles)
    )
    summed_grad = lax.psum(local_grad.reshape(logits.shape), "region")
    logit_grad = probs * (summed_grad - jnp.sum(probs * summed_grad, axis=-1, keepdims=True))
    return (logit_grad, usage_edges.reshape(capacity.shape))


def solution(mesh):
    in_specs = (
        P("nets", None),
        P("nets", "region", None, None, None),
        P("nets", "region", None),
        P("nets", "region", None),
        P("nets", "region", None),
        P("region", "nets"),
    )
    out_specs = (P("nets", None), P("region", "nets"))
    return jax.shard_map(shards, mesh=mesh, in_specs=in_specs, out_specs=out_specs, check_vma=False)
```

profile of v0, /device:TPU:0, one launch (start us, length us, event | category | flops | bytes accessed | tf_op | source)
XLA Modules:
  0.0 181.0 jit_solution(4683535861114849851)
XLA Ops:
  7.2 0.0 reduce-scatter.2.cloned.1.call-start
  7.2 0.7 fusion.17
  7.9 0.7 fusion.18
  8.6 1.4 reduce_max.9
  10.1 1.6 fusion.5
  11.7 0.7 fusion.16
  12.4 0.1 reshape.122
  12.5 1.6 fusion.21
  14.0 0.0 copy-start.1
  14.1 0.2 reshape.119
  14.2 1.4 gather_fusion
  15.7 6.4 %fusion.2 = f32[384,1,128]{2,1,0:T(1,128)S(1)} fusion(bf16[1,1,384,128,128]{4,3,2,1,0:T(8,128)(2,1)} %param.7, bf16[384,128,1]{1,0,2:T(8,128)(2,1)S(1)} %bitcast.18), kind=kOutput, calls=%fused_computation.6 | convolution fusion | flops 12582912 | bytes 12877824 | tf_op jit(solution)/shard_map/tq,tqe->te/dot_general | solution.py:24
  22.1 0.0 copy-start
  22.1 2.6 %scatter_custom_fusion = f32[512,128]{1,0:T(8,128)} fusion(s32[384]{0:T(512)S(1)} %fusion.18, f32[384,128]{1,0:T(8,128)S(1)} %bitcast.19, f32[]{:T(128)} %constant.11.clone.1, f32[384]{0:T(512)S(1)} %reshape.122), kind=kCustom, calls=%fused_computation.18 | custom fusion | flops 98304 | bytes 460804 | tf_op jit(solution)/shard_map/scatter-add | solution.py:32
  24.7 0.0 reduce-scatter.2.cloned.1.call-update
  24.7 0.0 all-reduce.2.cloned.1.call-start
  24.8 0.0 copy-done.1
  24.8 64.0 %reduce-scatter.2.cloned.1.call-done = f32[64,128]{1,0:T(8,128)} async-done(((f32[512,128]{1,0:T(8,128)}), f32[64,128]{1,0:T(8,128)}) %reduce-scatter.2.cloned.1.call-update) | async-done | bytes 32784 | tf_op jit(solution)/shard_map/reduce_scatter | solution.py:34
  88.8 0.8 divide_convert_fusion
  89.6 30.5 %all_gather.3 = bf16[512,128]{1,0:T(8,128)(2,1)S(1)} all-gather(bf16[64,128]{1,0:T(8,128)(2,1)S(1)} %divide_convert_fusion), channel_id=1, replica_groups=mesh['nets'=8,'region'=4] {'nets'}, dimensions={0}, use_global_device_ids=true | all-gather | bytes 147456 | tf_op jit(solution)/shard_map/all_gather | solution.py:36
  120.1 1.4 gather_fusion.1
  121.6 9.5 %fusion = f32[384,1,128]{2,1,0:T(1,128)S(1)} fusion(bf16[1,1,384,128,128]{4,3,2,1,0:T(8,128)(2,1)} %param.7, bf16[384,128,1]{1,0,2:T(8,128)(2,1)S(1)} %bitcast.20), kind=kOutput, calls=%fused_computation.4 | convolution fusion | flops 12582912 | bytes 12877824 | tf_op jit(solution)/shard_map/tqe,te->tq/dot_general | solution.py:39
  131.0 2.2 %scatter_custom_fusion.1 = f32[2048,128]{1,0:T(8,128)S(1)} fusion(s32[384]{0:T(512)S(1)} %fusion.17, f32[]{:T(128)} %constant.11.clone.1, f32[384,128]{1,0:T(8,128)S(1)} %bitcast.21, f32[384]{0:T(512)S(1)} %reshape.122), kind=kCustom, calls=%fused_computation.13 | custom fusion | flops 98304 | bytes 1247236 | tf_op jit(solution)/shard_map/scatter-add | solution.py:43
  133.2 1.3 reshape.120
  134.5 0.0 all-reduce.2.cloned.1.call-update
  134.5 35.3 %all-reduce.2.cloned.1.call-done = f32[1024,256]{1,0:T(8,128)} async-done(((f32[1024,256]{1,0:T(8,128)}), f32[1024,256]{1,0:T(8,128)}) %all-reduce.2.cloned.1.call-update) | async-done | bytes 1048592 | tf_op jit(solution)/shard_map/psum | solution.py:45
  169.8 0.0 copy-done
  169.8 1.7 multiply_reduce_fusion
  171.5 2.7 %subtract_multiply_fusion = f32[1024,256]{1,0:T(8,128)} fusion(f32[1024,256]{1,0:T(8,128)} %all-reduce.2.cloned.1.call-done, f32[1024]{0:T(1024)S(1)} %multiply_reduce_fusion, f32[1024]{0:T(1024)S(1)} %fusion.5, f32[1024,256]{1,0:T(8,128)S(1)} %copy-done, f32[1024]{0:T(1024)S(1)} %reduce_max.9), kind=kLoop, calls=%fused_computation.8 | loop fusion | flops 1048576 | bytes 3158016 | tf_op jit(solution)/shard_map/mul | solution.py:46
  (3 shorter events, 0.0 us)
Async XLA Ops:
  7.2 81.6 %reduce-scatter.2.cloned.1.call-start = ((), (), s32[]{:S(2)}) async-start(), calls=%async_computation.1 | async-start | bytes 294912 | tf_op jit(solution)/shard_map/reduce_scatter | solution.py:34
  14.0 10.7 %copy-start.1 = (s32[1,8192]{1,0:T(1,128)S(1)}, s32[1,8192]{1,0:T(1,128)}, u32[]{:S(2)}) copy-start(s32[1,8192]{1,0:T(1,128)} %param.11) | copy-start | bytes 98308
  22.1 147.8 %copy-start = (f32[1024,256]{1,0:T(8,128)S(1)}, f32[1024,256]{1,0:T(8,128)}, u32[]{:S(2)}) copy-start(f32[1024,256]{1,0:T(8,128)} %param.6) | copy-start | bytes 3145732
  24.7 145.1 %all-reduce.2.cloned.1.call-start = ((), (), s32[]{:S(2)}) async-start(), calls=%async_computation.2 | async-start | bytes 2097152 | tf_op jit(solution)/shard_map/psum | solution.py:45
Sparse Core Ops, SparseCore 0:
  24.8 63.9 reduce-scatter.1
  134.7 35.0 all-reduce.1
where the time goes:
time: 181 us
  waiting for transfers between devices  99.3 us (55%)
  blocking collectives  30.5 us (17%)
  other arithmetic  16.8 us (9%)
  matrix products  15.8 us (9%)
  between operations  14.1 us (8%)
  local copies, waits for them, and re-layouts  4.42 us (2%)
    reduce_scatter x1, waiting for transfers between devices, shards(): lax.psum_scatter(partial_value, 'nets', scatter_dimension=0, tiled=True)  64 us
    psum x1, waiting for transfers between devices, shards(): summed_grad = lax.psum(local_grad.reshape(logits.shape), 'region')  35.3 us
    all_gather x1, blocking collectives, shards(): all_grads = lax.all_gather(edge_grad, 'nets', axis=0, tiled=True)  30.5 us
    dot_general x1, matrix products, shards(): jnp.einsum('tqe,te->tq', tile_block, slot_grads, preferred_element_type=j...  9.46 us
    dot_general x1, matrix products, shards(): jnp.einsum('tq,tqe->te', picked, tile_block, preferred_element_type=jnp.f...  6.35 us
  transfers between devices with their start and end apart: 2, of which 2 were waited for; matrix products, arithmetic and copies ran while one was open for 0% of the time, Pallas kernels for 0%

commit v1 on v0

--- a/solution.py
+++ b/solution.py
@@ -33,7 +33,25 @@
     )
     usage_edges = lax.psum_scatter(partial_value, "nets", scatter_dimension=0, tiled=True)
     edge_grad = jax.nn.sigmoid(usage_edges - capacity_f).astype(jnp.bfloat16)
-    all_grads = lax.all_gather(edge_grad, "nets", axis=0, tiled=True)
+    size, index, width = (lax.axis_size("nets"), lax.axis_index("nets"), edge_grad.shape[0])
+    upward = [(i, (i + 1) % size) for i in range(size)]
+    backward = [(i, (i - 1) % size) for i in range(size)]
+    all_grads = jnp.zeros(
+        (*edge_grad.shape[:0], size * width, *edge_grad.shape[0 + 1 :]), edge_grad.dtype
+    )
+    all_grads = lax.dynamic_update_slice_in_dim(all_grads, edge_grad, index * width, axis=0)
+    from_left = from_right = edge_grad
+    halfway = size // 2
+    for step in range(1, halfway + 1):
+        from_left = lax.ppermute(from_left, "nets", upward)
+        all_grads = lax.dynamic_update_slice_in_dim(
+            all_grads, from_left, (index - step) % size * width, axis=0
+        )
+        if step < size - halfway:
+            from_right = lax.ppermute(from_right, "nets", backward)
+            all_grads = lax.dynamic_update_slice_in_dim(
+                all_grads, from_right, (index + step) % size * width, axis=0
+            )
     slot_grads = all_grads[target]
     dp_tiles = (
         jnp.einsum("tqe,te->tq", tile_block, slot_grads, preferred_element_type=jnp.float32)

time: 181 us -> 174 us (0.961)
  blocking collectives: 30.5 us -> 0 us
  starting transfers between devices: 0.08 us -> 14.3 us
  waiting for transfers between devices: 99.3 us -> 109 us
    all_gather x1 -> x0, blocking collectives: 30.5 us -> none  [shards(): all_grads = lax.all_gather(edge_grad, 'nets', axis=0, tiled=True)]
    ppermute x0 -> x7, starting transfers between devices: none -> 14.2 us  [the longest x3 12.7 us: shards(): from_right = lax.ppermute(from_right, 'nets', backward)]
    ppermute x0 -> x7, waiting for transfers between devices: none -> 11.6 us  [the longest x4 11.6 us: shards(): from_left = lax.ppermute(from_left, 'nets', upward)]
    psum x1, waiting for transfers between devices: 35.3 us -> 33.4 us  [shards(): summed_grad = lax.psum(local_grad.reshape(logits.shape), 'region')]
  transfers between devices with their start and end apart: 2 -> 9, of which waited for: 2 -> 6; matrix products, arithmetic and copies ran while one was open for 0% -> 0% of each run, Pallas kernels for 0% -> 0%
where the time goes in v1:
time: 174 us
  waiting for transfers between devices  109 us (63%)
  other arithmetic  16.1 us (9%)
  matrix products  15.8 us (9%)
  starting transfers between devices  14.3 us (8%)
  between operations  14.1 us (8%)
  local copies, waits for them, and re-layouts  4.5 us (3%)
    reduce_scatter x1, waiting for transfers between devices, shards(): lax.psum_scatter(partial_value, 'nets', scatter_dimension=0, tiled=True)  64 us
    psum x1, waiting for transfers between devices, shards(): summed_grad = lax.psum(local_grad.reshape(logits.shape), 'region')  33.4 us
    ppermute x3, starting transfers between devices, shards(): from_right = lax.ppermute(from_right, 'nets', backward)  12.7 us
    ppermute x4, waiting for transfers between devices, shards(): from_left = lax.ppermute(from_left, 'nets', upward)  11.6 us
    dot_general x1, matrix products, shards(): jnp.einsum('tqe,te->tq', tile_block, slot_grads, preferred_element_type=j...  9.46 us
    dot_general x1, matrix products, shards(): jnp.einsum('tq,tqe->te', picked, tile_block, preferred_element_type=jnp.f...  6.35 us
  transfers between devices with their start and end apart: 9, of which 6 were waited for; matrix products, arithmetic and copies ran while one was open for 0% of the time, Pallas kernels for 0%

profile of v1, /device:TPU:0, one launch (start us, length us, event | category | flops | bytes accessed | tf_op | source)
XLA Modules:
  0.0 173.9 jit_solution(13941080090100039906)
XLA Ops:
  7.2 0.0 reduce-scatter.2.cloned.1.call-start
  7.2 1.4 reduce_max.9
  8.7 1.6 fusion.5
  10.2 0.7 fusion.16
  11.0 0.1 reshape.122
  11.0 0.7 fusion.17
  11.8 1.6 fusion.21
  13.4 0.0 copy-start.1
  13.4 0.2 reshape.119
  13.6 1.4 gather_fusion
  15.0 6.4 %fusion.2 = f32[384,1,128]{2,1,0:T(1,128)S(1)} fusion(bf16[1,1,384,128,128]{4,3,2,1,0:T(8,128)(2,1)} %param.7, bf16[384,128,1]{1,0,2:T(8,128)(2,1)S(1)} %bitcast.18), kind=kOutput, calls=%fused_computation.6 | convolution fusion | flops 12582912 | bytes 12877824 | tf_op jit(solution)/shard_map/tq,tqe->te/dot_general | solution.py:24
  21.4 0.0 copy-start
  21.4 2.6 %scatter_custom_fusion = f32[512,128]{1,0:T(8,128)} fusion(s32[384]{0:T(512)S(1)} %get-tuple-element.5, f32[384,128]{1,0:T(8,128)S(1)} %bitcast.19, f32[]{:T(128)} %constant.68.clone.1, f32[384]{0:T(512)S(1)} %reshape.122), kind=kCustom, calls=%fused_computation.18 | custom fusion | flops 98304 | bytes 460804 | tf_op jit(solution)/shard_map/scatter-add | solution.py:32
  24.0 0.0 reduce-scatter.2.cloned.1.call-update
  24.0 0.0 all-reduce.2.cloned.1.call-start
  24.1 0.0 copy-done.1
  24.1 64.0 %reduce-scatter.2.cloned.1.call-done = f32[64,128]{1,0:T(8,128)} async-done(((f32[512,128]{1,0:T(8,128)}), f32[64,128]{1,0:T(8,128)}) %reduce-scatter.2.cloned.1.call-update) | async-done | bytes 32784 | tf_op jit(solution)/shard_map/reduce_scatter | solution.py:34
  88.1 0.8 constant_dynamic-update-slice_fusion.7
  88.9 1.5 collective-permute-start
  90.4 3.3 %collective-permute-start.1 = (bf16[64,128]{1,0:T(8,128)(2,1)S(1)}, bf16[64,128]{1,0:T(8,128)(2,1)S(1)}, u32[]{:S(2)}, u32[]{:S(2)}) collective-permute-start(bf16[64,128]{1,0:T(8,128)(2,1)S(1)} %get-tuple-element.3), channel_id=1, source_target_pairs={{0,28},{4,0},{8,4},{12,8},{16,12},{20,16},{24,20},{28,24},{1,29},{... | collective-permute-start | bytes 49160 | tf_op jit(solution)/shard_map/ppermute | solution.py:51
  93.7 1.7 collective-permute-done
  95.4 0.0 collective-permute-start.2
  95.4 0.0 collective-permute-done.1
  95.4 4.7 %collective-permute-start.3 = (bf16[64,128]{1,0:T(8,128)(2,1)S(1)}, bf16[64,128]{1,0:T(8,128)(2,1)S(1)}, u32[]{:S(2)}, u32[]{:S(2)}) collective-permute-start(bf16[64,128]{1,0:T(8,128)(2,1)S(1)} %collective-permute-done.1), channel_id=1, source_target_pairs={{0,28},{4,0},{8,4},{12,8},{16,12},{20,16},{24,20},{28,24},{1,29},{... | collective-permute-start | bytes 49160 | tf_op jit(solution)/shard_map/ppermute | solution.py:51
  100.2 1.7 collective-permute-done.2
  101.9 0.0 collective-permute-start.4
  101.9 0.0 collective-permute-done.3
  101.9 4.7 %collective-permute-start.5 = (bf16[64,128]{1,0:T(8,128)(2,1)S(1)}, bf16[64,128]{1,0:T(8,128)(2,1)S(1)}, u32[]{:S(2)}, u32[]{:S(2)}) collective-permute-start(bf16[64,128]{1,0:T(8,128)(2,1)S(1)} %collective-permute-done.3), channel_id=1, source_target_pairs={{0,28},{4,0},{8,4},{12,8},{16,12},{20,16},{24,20},{28,24},{1,29},{... | collective-permute-start | bytes 49160 | tf_op jit(solution)/shard_map/ppermute | solution.py:51
  106.6 1.8 %collective-permute-done.4 = bf16[64,128]{1,0:T(8,128)(2,1)S(1)} collective-permute-done((bf16[64,128]{1,0:T(8,128)(2,1)S(1)}, bf16[64,128]{1,0:T(8,128)(2,1)S(1)}, u32[]{:S(2)}, u32[]{:S(2)}) %collective-permute-start.4) | collective-permute-done | bytes 16416 | tf_op jit(solution)/shard_map/ppermute | solution.py:46
  108.4 0.0 collective-permute-start.6
  108.4 0.0 collective-permute-done.5
  108.5 6.4 %collective-permute-done.6 = bf16[64,128]{1,0:T(8,128)(2,1)S(1)} collective-permute-done((bf16[64,128]{1,0:T(8,128)(2,1)S(1)}, bf16[64,128]{1,0:T(8,128)(2,1)S(1)}, u32[]{:S(2)}, u32[]{:S(2)}) %collective-permute-start.6) | collective-permute-done | bytes 16416 | tf_op jit(solution)/shard_map/ppermute | solution.py:46
  114.9 1.4 gather_fusion.1
  116.3 9.5 %fusion = f32[384,1,128]{2,1,0:T(1,128)S(1)} fusion(bf16[1,1,384,128,128]{4,3,2,1,0:T(8,128)(2,1)} %param.7, bf16[384,128,1]{1,0,2:T(8,128)(2,1)S(1)} %bitcast.20), kind=kOutput, calls=%fused_computation.4 | convolution fusion | flops 12582912 | bytes 12877824 | tf_op jit(solution)/shard_map/tqe,te->tq/dot_general | solution.py:57
  125.8 2.2 %scatter_custom_fusion.1 = f32[2048,128]{1,0:T(8,128)S(1)} fusion(s32[384]{0:T(512)S(1)} %get-tuple-element.4, f32[]{:T(128)} %constant.68.clone.1, f32[384,128]{1,0:T(8,128)S(1)} %bitcast.21, f32[384]{0:T(512)S(1)} %reshape.122), kind=kCustom, calls=%fused_computation.13 | custom fusion | flops 98304 | bytes 1247236 | tf_op jit(solution)/shard_map/scatter-add | solution.py:61
  128.0 1.3 reshape.120
  129.3 0.0 all-reduce.2.cloned.1.call-update
  129.3 33.4 %all-reduce.2.cloned.1.call-done = f32[1024,256]{1,0:T(8,128)} async-done(((f32[1024,256]{1,0:T(8,128)}), f32[1024,256]{1,0:T(8,128)}) %all-reduce.2.cloned.1.call-update) | async-done | bytes 1048592 | tf_op jit(solution)/shard_map/psum | solution.py:63
  162.7 0.0 copy-done
  162.7 1.7 multiply_reduce_fusion
  164.4 2.7 %subtract_multiply_fusion = f32[1024,256]{1,0:T(8,128)} fusion(f32[1024,256]{1,0:T(8,128)} %all-reduce.2.cloned.1.call-done, f32[1024]{0:T(1024)S(1)} %multiply_reduce_fusion, f32[1024]{0:T(1024)S(1)} %fusion.5, f32[1024,256]{1,0:T(8,128)S(1)} %copy-done, f32[1024]{0:T(1024)S(1)} %reduce_max.9), kind=kLoop, calls=%fused_computation.8 | loop fusion | flops 1048576 | bytes 3158016 | tf_op jit(solution)/shard_map/mul | solution.py:64
  (11 shorter events, 0.1 us)
Async XLA Ops:
  7.2 81.0 %reduce-scatter.2.cloned.1.call-start = ((), (), s32[]{:S(2)}) async-start(), calls=%async_computation.1 | async-start | bytes 294912 | tf_op jit(solution)/shard_map/reduce_scatter | solution.py:34
  13.4 10.7 %copy-start.1 = (s32[1,8192]{1,0:T(1,128)S(1)}, s32[1,8192]{1,0:T(1,128)}, u32[]{:S(2)}) copy-start(s32[1,8192]{1,0:T(1,128)} %param.11) | copy-start | bytes 98308
  21.4 141.3 %copy-start = (f32[1024,256]{1,0:T(8,128)S(1)}, f32[1024,256]{1,0:T(8,128)}, u32[]{:S(2)}) copy-start(f32[1024,256]{1,0:T(8,128)} %param.6) | copy-start | bytes 3145732
  24.0 138.7 %all-reduce.2.cloned.1.call-start = ((), (), s32[]{:S(2)}) async-start(), calls=%async_computation.2 | async-start | bytes 2097152 | tf_op jit(solution)/shard_map/psum | solution.py:63
  88.9 6.5 %collective-permute-start = (bf16[64,128]{1,0:T(8,128)(2,1)S(1)}, bf16[64,128]{1,0:T(8,128)(2,1)S(1)}, u32[]{:S(2)}, u32[]{:S(2)}) collective-permute-start(bf16[64,128]{1,0:T(8,128)(2,1)S(1)} %get-tuple-element.3), channel_id=1, source_target_pairs={{0,4},{4,8},{8,12},{12,16},{16,20},{20,24},{24,28},{28,0},{1,5},{5... | collective-permute-start | bytes 49160 | tf_op jit(solution)/shard_map/ppermute | solution.py:46
  90.4 5.0 %collective-permute-start.1 = (bf16[64,128]{1,0:T(8,128)(2,1)S(1)}, bf16[64,128]{1,0:T(8,128)(2,1)S(1)}, u32[]{:S(2)}, u32[]{:S(2)}) collective-permute-start(bf16[64,128]{1,0:T(8,128)(2,1)S(1)} %get-tuple-element.3), channel_id=1, source_target_pairs={{0,28},{4,0},{8,4},{12,8},{16,12},{20,16},{24,20},{28,24},{1,29},{... | collective-permute-start | bytes 49160 | tf_op jit(solution)/shard_map/ppermute | solution.py:51
  95.4 6.4 %collective-permute-start.2 = (bf16[64,128]{1,0:T(8,128)(2,1)S(1)}, bf16[64,128]{1,0:T(8,128)(2,1)S(1)}, u32[]{:S(2)}, u32[]{:S(2)}) collective-permute-start(bf16[64,128]{1,0:T(8,128)(2,1)S(1)} %collective-permute-done), channel_id=1, source_target_pairs={{0,4},{4,8},{8,12},{12,16},{16,20},{20,24},{24,28},{28,0},{1,5},{5... | collective-permute-start | bytes 49160 | tf_op jit(solution)/shard_map/ppermute | solution.py:46
  95.4 6.4 %collective-permute-start.3 = (bf16[64,128]{1,0:T(8,128)(2,1)S(1)}, bf16[64,128]{1,0:T(8,128)(2,1)S(1)}, u32[]{:S(2)}, u32[]{:S(2)}) collective-permute-start(bf16[64,128]{1,0:T(8,128)(2,1)S(1)} %collective-permute-done.1), channel_id=1, source_target_pairs={{0,28},{4,0},{8,4},{12,8},{16,12},{20,16},{24,20},{28,24},{1,29},{... | collective-permute-start | bytes 49160 | tf_op jit(solution)/shard_map/ppermute | solution.py:51
  101.9 6.6 %collective-permute-start.4 = (bf16[64,128]{1,0:T(8,128)(2,1)S(1)}, bf16[64,128]{1,0:T(8,128)(2,1)S(1)}, u32[]{:S(2)}, u32[]{:S(2)}) collective-permute-start(bf16[64,128]{1,0:T(8,128)(2,1)S(1)} %collective-permute-done.2), channel_id=1, source_target_pairs={{0,4},{4,8},{8,12},{12,16},{16,20},{20,24},{24,28},{28,0},{1,5},{5... | collective-permute-start | bytes 49160 | tf_op jit(solution)/shard_map/ppermute | solution.py:46
  101.9 6.6 %collective-permute-start.5 = (bf16[64,128]{1,0:T(8,128)(2,1)S(1)}, bf16[64,128]{1,0:T(8,128)(2,1)S(1)}, u32[]{:S(2)}, u32[]{:S(2)}) collective-permute-start(bf16[64,128]{1,0:T(8,128)(2,1)S(1)} %collective-permute-done.3), channel_id=1, source_target_pairs={{0,28},{4,0},{8,4},{12,8},{16,12},{20,16},{24,20},{28,24},{1,29},{... | collective-permute-start | bytes 49160 | tf_op jit(solution)/shard_map/ppermute | solution.py:51
  108.4 6.4 %collective-permute-start.6 = (bf16[64,128]{1,0:T(8,128)(2,1)S(1)}, bf16[64,128]{1,0:T(8,128)(2,1)S(1)}, u32[]{:S(2)}, u32[]{:S(2)}) collective-permute-start(bf16[64,128]{1,0:T(8,128)(2,1)S(1)} %collective-permute-done.4), channel_id=1, source_target_pairs={{0,4},{4,8},{8,12},{12,16},{16,20},{20,24},{24,28},{28,0},{1,5},{5... | collective-permute-start | bytes 49160 | tf_op jit(solution)/shard_map/ppermute | solution.py:46
Sparse Core Ops, SparseCore 0:
  24.1 63.9 reduce-scatter.1
  129.4 33.2 all-reduce.1
